TPU v7x, 256 devices: a whole 4x4x8 slice. The times are simulated.
256 devices in a mesh: req: 32 (over x, y, core), tp: 8 (over z).
Axes of the slice: x: 4, y: 4, z: 8, core: 2. Of those that a mesh axis runs over, the one named last changes fastest.
Arguments:
- query: bfloat16 [768, 4096], P('req', 'tp'), may hold values from -102 to 102
- new_key: bfloat16 [768, 1024], P('req', 'tp'), may hold values from -6 to 6
- new_value: bfloat16 [768, 1024], P('req', 'tp'), may hold values from -6 to 6
- prefix_key: bfloat16 [64, 6144, 1024], P('req', None, 'tp'), may hold values from -6 to 6
- prefix_value: bfloat16 [64, 6144, 1024], P('req', None, 'tp'), may hold values from -6 to 6
- suffix_key: bfloat16 [768, 128, 1024], P('req', None, 'tp'), may hold values from -6 to 6
- suffix_value: bfloat16 [768, 128, 1024], P('req', None, 'tp'), may hold values from -6 to 6
- group_ids: int32 [768], replicated, may hold values from 0 to 63, as said below
- prompt_len: int32 [64], P('req'), may hold values from 768 to 6144, as said below
- suffix_len: int32 [768], replicated, may hold values from 1 to 128, as said below
- o_weight: bfloat16 [4096, 4096], P('tp'), may hold values from -0.09375 to 0.09375
- residual: bfloat16 [768, 4096], P('req'), may hold values from -0.29882812 to 0.29882812
- norm_gain: bfloat16 [4096], replicated, may hold values from 0.5 to 1.5
Outputs:
- hidden: bfloat16 [768, 4096], P('req')
- normed: bfloat16 [768, 4096], P('req')
Inputs may be any that keep to these rules, and one draw needn't show every extreme that they name: Request r belongs to group group_ids[r]; groups 2k to 2k + 1 at a time are held together (group // 2 names the holder). Among each aligned block of 24 requests, every holder that appears is named by exactly 2 of them. `prompt_len`: some group has exactly 6144. `suffix_len`: some request has exactly 128.
All inputs are finite; a program needn't handle non-finite values.
Results may differ from a plain program's by a relative error of at most 0.008.
Values may be sent and summed in bfloat16 or wider, within the bound.
No kernel may reach another device: no remote copies, remote signals or barrier semaphores. Data moves between devices by JAX's collectives and lax.ppermute only.
A program may use at most 64 MiB of HBM per device.

v0:
```python
import math
import jax
import jax.numpy as jnp
from jax import lax
from jax.sharding import PartitionSpec as P

HD = 128
WIN = 4096
SINKS = 4
FAR_BELOW = -1e30
NORM_EPS = 1e-06


def prefix_attend(
    rows_query, row_group, row_suffix, prefix_key, prefix_value, prompt_len, first_group, blocks
):
    row_count = rows_query.shape[0]
    groups_dev = prefix_key.shape[0]
    prompt_max = prefix_key.shape[1]
    kv_dev = prefix_key.shape[2] // HD
    heads_dev = rows_query.shape[1] // HD
    repeat = heads_dev // kv_dev
    block_len = min(512, prompt_max)
    score_scale = 1.0 / math.sqrt(HD)
    local_group = row_group - first_group
    owned = (local_group >= 0) & (local_group < groups_dev)
    member = local_group[:, None] == jnp.arange(groups_dev, dtype=jnp.int32)[None, :]
    row_prompt = jnp.sum(jnp.where(member, prompt_len[None, :], 0), axis=1)
    row_low = row_prompt + row_suffix - WIN + 1
    queries = rows_query.reshape(row_count, kv_dev, repeat, HD)

    def key_step(block_index, loop_state):
        running, weight_sum, weighted = loop_state
        key_start = block_index * block_len
        key_block = lax.dynamic_slice_in_dim(prefix_key, key_start, block_len, 1).reshape(
            groups_dev, block_len, kv_dev, HD
        )
        value_block = lax.dynamic_slice_in_dim(prefix_value, key_start, block_len, 1).reshape(
            groups_dev, block_len, kv_dev, HD
        )
        scores = (
            jnp.einsum("rkhd,gpkd->rkhgp", queries, key_block, preferred_element_type=jnp.float32)
            * score_scale
        )
        positions = key_start + jnp.arange(block_len, dtype=jnp.int32)
        inside = positions[None, :] < prompt_len[:, None]
        window = (positions[None, :] < SINKS) | (positions[None, :] >= row_low[:, None])
        usable = member[:, :, None] & inside[None, :, :] & window[:, None, :]
        usable = usable[:, None, None, :, :]
        masked = jnp.where(usable, scores, FAR_BELOW)
        updated = jnp.maximum(running, jnp.max(masked, axis=(3, 4)))
        weights = jnp.where(usable, jnp.exp(masked - updated[..., None, None]), 0.0)
        rescale = jnp.exp(running - updated)
        weight_sum = weight_sum * rescale + jnp.sum(weights, axis=(3, 4))
        rounded = weights.astype(jnp.bfloat16)
        weighted = weighted * rescale[..., None] + jnp.einsum(
            "rkhgp,gpkd->rkhd", rounded, value_block, preferred_element_type=jnp.float32
        )
        return (updated, weight_sum, weighted)

    initial = (
        jnp.full((row_count, kv_dev, repeat), FAR_BELOW, jnp.float32),
        jnp.zeros((row_count, kv_dev, repeat), jnp.float32),
        jnp.zeros((row_count, kv_dev, repeat, HD), jnp.float32),
    )
    running, weight_sum, weighted = lax.fori_loop(0, blocks, key_step, initial)
    bounded = jnp.maximum(weight_sum, 1.0)
    normalized = jnp.where(owned[:, None, None, None], weighted / bounded[..., None], 0.0).reshape(
        row_count, heads_dev * HD
    )
    log_total = jnp.where(owned[:, None, None], running + jnp.log(bounded), 0.0).reshape(
        row_count, heads_dev
    )
    return (normalized, log_total)


def body(
    query,
    new_key,
    new_value,
    prefix_key,
    prefix_value,
    suffix_key,
    suffix_value,
    group_ids,
    prompt_len,
    suffix_len,
    o_weight,
    residual,
    norm_gain,
):
    req_dev = query.shape[0]
    heads_dev = query.shape[1] // HD
    kv_dev = new_key.shape[1] // HD
    repeat = heads_dev // kv_dev
    groups_dev = prefix_key.shape[0]
    prompt_max = prefix_key.shape[1]
    suffix_max = suffix_key.shape[1]
    block_len = min(512, prompt_max)
    score_scale = 1.0 / math.sqrt(HD)
    places = lax.axis_size("req")
    device = lax.axis_index("req")
    first_group = device * groups_dev
    own_suffix = lax.dynamic_slice_in_dim(suffix_len, device * req_dev, req_dev)
    blocks = prompt_max // block_len
    capacity = max(2, req_dev // places)
    slot_total = places * capacity
    all_groups = group_ids.reshape(places, 1, req_dev)
    all_suffix = suffix_len.reshape(places, 1, req_dev)
    all_rows = (
        jnp.arange(places, dtype=jnp.int32)[:, None] * req_dev
        + jnp.arange(req_dev, dtype=jnp.int32)[None, :]
    ).reshape(places, 1, req_dev)
    is_mine = (group_ids // groups_dev).reshape(places, req_dev) == device
    slot_order = jnp.cumsum(is_mine.astype(jnp.int32), axis=1) - 1
    slot_pick = is_mine[:, None, :] & (
        slot_order[:, None, :] == jnp.arange(capacity, dtype=jnp.int32)[None, :, None]
    )
    filled = jnp.any(slot_pick, axis=2)
    slot_group = jnp.where(
        filled, jnp.sum(jnp.where(slot_pick, all_groups, 0), axis=2), -1
    ).reshape(slot_total)
    slot_suffix = jnp.sum(jnp.where(slot_pick, all_suffix, 0), axis=2).reshape(slot_total)
    slot_row = jnp.where(filled, jnp.sum(jnp.where(slot_pick, all_rows, 0), axis=2), -1).reshape(
        slot_total
    )
    every_query = lax.all_gather(query, "req", axis=0, tiled=True)
    pick_rows = slot_row[:, None] == jnp.arange(places * req_dev, dtype=jnp.int32)[None, :]
    compact = jnp.dot(
        pick_rows.astype(jnp.bfloat16), every_query, preferred_element_type=jnp.float32
    ).astype(jnp.bfloat16)
    part_out, part_log = prefix_attend(
        compact, slot_group, slot_suffix, prefix_key, prefix_value, prompt_len, first_group, blocks
    )
    spread_rows = pick_rows.T.astype(jnp.float32)
    spread_out = jnp.dot(spread_rows, part_out, precision=lax.Precision.HIGHEST)
    spread_log = jnp.dot(spread_rows, part_log, precision=lax.Precision.HIGHEST)
    prefix_out, prefix_log = (
        lax.psum_scatter(spread_out, "req", scatter_dimension=0, tiled=True),
        lax.psum_scatter(spread_log, "req", scatter_dimension=0, tiled=True),
    )
    queries = query.reshape(req_dev, kv_dev, repeat, HD)
    key_rows = suffix_key.reshape(req_dev, suffix_max, kv_dev, HD)
    value_rows = suffix_value.reshape(req_dev, suffix_max, kv_dev, HD)
    scores = (
        jnp.einsum("rkhd,rjkd->rkhj", queries, key_rows, preferred_element_type=jnp.float32)
        * score_scale
    )
    own_score = (
        jnp.einsum(
            "rkhd,rkd->rkh",
            queries,
            new_key.reshape(req_dev, kv_dev, HD),
            preferred_element_type=jnp.float32,
        )
        * score_scale
    )
    usable = (jnp.arange(suffix_max, dtype=jnp.int32)[None, :] < own_suffix[:, None])[
        :, None, None, :
    ]
    masked = jnp.where(usable, scores, FAR_BELOW)
    running = jnp.maximum(jnp.max(masked, axis=-1), own_score)
    weights = jnp.where(usable, jnp.exp(masked - running[..., None]), 0.0)
    own_weight = jnp.exp(own_score - running)
    weight_sum = jnp.sum(weights, axis=-1) + own_weight
    weighted = jnp.einsum(
        "rkhj,rjkd->rkhd",
        weights.astype(jnp.bfloat16),
        value_rows,
        preferred_element_type=jnp.float32,
    )
    own_rounded = own_weight.astype(jnp.bfloat16).astype(jnp.float32)
    weighted = weighted + own_rounded[..., None] * new_value.reshape(req_dev, kv_dev, 1, HD).astype(
        jnp.float32
    )
    local_out = weighted / weight_sum[..., None]
    local_log = running + jnp.log(weight_sum)
    prefix_out = prefix_out.reshape(req_dev, kv_dev, repeat, HD)
    prefix_log = prefix_log.reshape(req_dev, kv_dev, repeat)
    combined = jnp.logaddexp(prefix_log, local_log)
    attended = (
        prefix_out * jnp.exp(prefix_log - combined)[..., None]
        + local_out * jnp.exp(local_log - combined)[..., None]
    )
    attended = attended.reshape(req_dev, heads_dev * HD).astype(jnp.bfloat16)
    partial_value = jnp.dot(attended, o_weight, preferred_element_type=jnp.float32)
    proj = lax.psum(partial_value, "tp")
    summed = residual.astype(jnp.float32) + proj
    hidden = summed.astype(jnp.bfloat16)
    inverse = lax.rsqrt(jnp.mean(summed * summed, axis=-1, keepdims=True) + NORM_EPS)
    normed = (summed * inverse * norm_gain.astype(jnp.float32)[None, :]).astype(jnp.bfloat16)
    return (hidden, normed)


def solution(mesh):
    placed = (
        P("req", "tp"),
        P("req", "tp"),
        P("req", "tp"),
        P("req", None, "tp"),
        P("req", None, "tp"),
        P("req", None, "tp"),
        P("req", None, "tp"),
        P(),
        P("req"),
        P(),
        P("tp", None),
        P("req", None),
        P(),
    )
    return jax.shard_map(
        body,
        mesh=mesh,
        in_specs=placed,
        out_specs=(P("req", None), P("req", None)),
        check_vma=False,
    )
```

profile of v0, /device:TPU:2, one launch (start us, length us, event | category | flops | bytes accessed | tf_op | source)
XLA Modules:
  0.0 305.6 jit_solution(10688126659396240701)
XLA Ops:
  11.4 24.9 %all_gather.3 = bf16[768,512]{1,0:T(8,128)(2,1)S(1)} all-gather(bf16[24,512]{1,0:T(8,128)(2,1)} %param.15), channel_id=1, replica_groups=mesh['req'=32,'tp'=8] {'req'}, dimensions={0}, use_global_device_ids=true | all-gather | bytes 811008 | tf_op jit(solution)/shard_map/all_gather | solution.py:127
  36.8 50.0 %while.18 = (s32[]{:T(128)}, f32[64,1,4]{0,2,1:T(4,128)S(1)}, f32[64,1,4]{0,2,1:T(4,128)S(1)}, f32[64,1,4,128]{3,0,2,1:T(8,128)S(1)}, s32[2]{0:T(128)}, /*index=...) while((s32[]{:T(128)}, f32[64,1,4]{0,2,1:T(4,128)S(1)}, ...), condition=%wide.region_9.10_spmd.clone, body=%wide.region_6.9_spmd.clone.sunk | while | flops 136876160 | bytes 4351967 | solution.py:66
  37.8 1.4 fusion.83
  39.6 1.4 fusion.86
  42.0 1.4 fusion.83
  43.8 1.4 fusion.86
  47.9 1.4 fusion.86
  52.1 1.4 fusion.86
  56.3 1.4 fusion.86
  58.7 1.4 fusion.83
  60.5 1.4 fusion.86
  62.9 1.4 fusion.83
  64.6 1.4 fusion.86
  68.8 1.4 fusion.86
  73.0 1.4 fusion.86
  77.1 1.4 fusion.86
  81.3 1.4 fusion.86
  83.7 1.4 fusion.83
  85.5 1.4 fusion.86
  87.2 2.0 fusion.27
  91.6 109.0 %all-reduce = f32[768,4]{0,1:T(4,128)S(1)} all-reduce(f32[768,4]{0,1:T(4,128)S(1)} %fusion.26), channel_id=3, replica_groups=mesh['req'=32,'tp'=8] {'req'}, use_global_device_ids=true, to_apply=%region_11.12.clone | all-reduce | flops 3072 | bytes 24576
  203.2 3.6 %fusion.37 = f32[24,4096]{1,0:T(8,128)} fusion(bf16[512,4096]{1,0:T(8,128)(2,1)} %param.25, bf16[3,8,4,128]{3,2,1,0:T(4,128)(2,1)S(1)} %bitcast.93), kind=kOutput, calls=%fused_computation.57 | convolution fusion | flops 100663296 | bytes 4612096 | tf_op jit(solution)/shard_map/dot_general | solution.py:186
  206.8 88.9 %all-reduce.3.cloned.1.call-done = f32[24,4096]{1,0:T(8,128)} async-done(((f32[24,4096]{1,0:T(8,128)}), f32[24,4096]{1,0:T(8,128)}) %all-reduce.3.cloned.1.call-update) | async-done | bytes 393232 | tf_op jit(solution)/shard_map/psum | solution.py:187
  297.0 1.8 multiply_convert_fusion
  (201 shorter events, 35.8 us)
Async XLA Ops:
  7.2 193.8 %copy-start = (bf16[24,128,128]{2,1,0:T(8,128)(2,1)S(1)}, bf16[24,128,128]{2,1,0:T(8,128)(2,1)}, u32[]{:S(2)}) copy-start(bf16[24,128,128]{2,1,0:T(8,128)(2,1)} %param.20) | copy-start | bytes 2359300
  7.2 194.8 %reduce-scatter.3.cloned.1.call-start = ((), (), s32[]{:S(2)}) async-start(), calls=%async_computation.1 | async-start | bytes 1622016 | tf_op jit(solution)/shard_map/reduce_scatter | solution.py:139
  86.9 2.4 copy-start.2
  86.9 3.2 %copy-start.7 = (u32[256]{0:T(256)S(1)}, u32[256]{0:T(256)}, u32[]{:S(2)}) copy-start(u32[256]{0:T(256)} %constant.130) | copy-start | bytes 3076
  86.9 113.9 %copy-start.4 = (bf16[24,128]{1,0:T(8,128)(2,1)S(1)}, bf16[24,128]{1,0:T(8,128)(2,1)}, u32[]{:S(2)}) copy-start(bf16[24,128]{1,0:T(8,128)(2,1)} %param.17) | copy-start | bytes 18436
  86.9 113.9 %copy-start.6 = (bf16[24,128]{1,0:T(8,128)(2,1)S(1)}, bf16[24,128]{1,0:T(8,128)(2,1)}, u32[]{:S(2)}) copy-start(bf16[24,128]{1,0:T(8,128)(2,1)} %param.16) | copy-start | bytes 18436
  86.9 115.8 %copy-start.5 = (bf16[24,128,128]{2,1,0:T(8,128)(2,1)S(1)}, bf16[24,128,128]{2,1,0:T(8,128)(2,1)}, u32[]{:S(2)}) copy-start(bf16[24,128,128]{2,1,0:T(8,128)(2,1)} %param.21) | copy-start | bytes 2359300
  89.2 206.5 %all-reduce.3.cloned.1.call-start = ((), (), s32[]{:S(2)}) async-start(), calls=%async_computation.2 | async-start | bytes 786432 | tf_op jit(solution)/shard_map/psum | solution.py:187
  202.8 4.0 %copy-start.3 = (bf16[4096]{0:T(1024)(128)(2,1)S(1)}, bf16[4096]{0:T(1024)(128)(2,1)}, u32[]{:S(2)}) copy-start(bf16[4096]{0:T(1024)(128)(2,1)} %param.27) | copy-start | bytes 24580
  202.8 93.0 %copy-start.1 = (bf16[24,4096]{1,0:T(8,128)(2,1)S(1)}, bf16[24,4096]{1,0:T(8,128)(2,1)}, u32[]{:S(2)}) copy-start(bf16[24,4096]{1,0:T(8,128)(2,1)} %param.26) | copy-start | bytes 589828
Sparse Core Ops, SparseCore 0:
  89.4 86.8 reduce-scatter.2
  206.9 88.8 all-reduce.2
where the time goes:
time: 307 us; the launch traced here: 306 us
  blocking collectives  134 us (44%)
  waiting for transfers between devices  89 us (29%)
  matrix products  40.4 us (13%)
  other arithmetic  21.3 us (7%)
  between operations  15 us (5%)
  local copies, waits for them, and re-layouts  5.04 us (2%)
    unnamed x1, blocking collectives  109 us
    psum x1, waiting for transfers between devices, body(): proj = lax.psum(partial_value, 'tp')  88.9 us
    all_gather x1, blocking collectives, body(): every_query = lax.all_gather(query, 'req', axis=0, tiled=True)  24.9 us
    dot_general x12, matrix products, key_step(): jnp.einsum('rkhgp,gpkd->rkhd', rounded, value_block, preferred_element_ty...  16.8 us
    dot_general x12, matrix products, key_step(): jnp.einsum('rkhd,gpkd->rkhgp', queries, key_block, preferred_element_type...  16.3 us
    lt x12, other arithmetic, key_step(): inside = positions[None, :] < prompt_len[:, None]  8.77 us
  transfers between devices with their start and end apart: 2, of which 1 were waited for; matrix products, arithmetic and copies ran while one was open for 1% of the time, Pallas kernels for 0%

commit v1 on v0

--- a/solution.py
+++ b/solution.py
@@ -9,6 +9,10 @@
 SINKS = 4
 FAR_BELOW = -1e30
 NORM_EPS = 1e-06
+
+
+def copies_take(in_array, mesh_dim):
+    return jnp.sum(lax.all_gather(in_array, axis_name=mesh_dim), 0)
 
 
 def prefix_attend(
@@ -184,7 +188,7 @@
     )
     attended = attended.reshape(req_dev, heads_dev * HD).astype(jnp.bfloat16)
     partial_value = jnp.dot(attended, o_weight, preferred_element_type=jnp.float32)
-    proj = lax.psum(partial_value, "tp")
+    proj = copies_take(partial_value, "tp")
     summed = residual.astype(jnp.float32) + proj
     hidden = summed.astype(jnp.bfloat16)
     inverse = lax.rsqrt(jnp.mean(summed * summed, axis=-1, keepdims=True) + NORM_EPS)

time: 307 us -> 279 us (0.909)
  waiting for transfers between devices: 89 us -> 60.7 us
    psum x1 -> x0, waiting for transfers between devices: 88.9 us -> none  [body(): proj = lax.psum(partial_value, 'tp')]
    all_gather x0 -> x1, waiting for transfers between devices: none -> 60.7 us  [copies_take(): return jnp.sum(lax.all_gather(in_array, axis_name=mesh_dim), 0)]
where the time goes in v1:
time: 279 us; the launch traced here: 277 us
  blocking collectives  134 us (48%)
  waiting for transfers between devices  60.7 us (22%)
  matrix products  40.3 us (14%)
  other arithmetic  21.3 us (8%)
  between operations  15 us (5%)
  local copies, waits for them, and re-layouts  5.04 us (2%)
    unnamed x1, blocking collectives  109 us
    all_gather x1, waiting for transfers between devices, copies_take(): return jnp.sum(lax.all_gather(in_array, axis_name=mesh_dim), 0)  60.7 us
    all_gather x1, blocking collectives, body(): every_query = lax.all_gather(query, 'req', axis=0, tiled=True)  24.9 us
    dot_general x12, matrix products, key_step(): jnp.einsum('rkhgp,gpkd->rkhd', rounded, value_block, preferred_element_ty...  16.7 us
    dot_general x12, matrix products, key_step(): jnp.einsum('rkhd,gpkd->rkhgp', queries, key_block, preferred_element_type...  16.3 us
    lt x12, other arithmetic, key_step(): inside = positions[None, :] < prompt_len[:, None]  8.77 us
  transfers between devices with their start and end apart: 2, of which 1 were waited for; matrix products, arithmetic and copies ran while one was open for 1% of the time, Pallas kernels for 0%

profile of v1, /device:TPU:2, one launch (start us, length us, event | category | flops | bytes accessed | tf_op | source)
XLA Modules:
  0.0 277.4 jit_solution(13008412157565895615)
XLA Ops:
  11.6 24.9 %all_gather.9 = bf16[768,512]{1,0:T(8,128)(2,1)S(1)} all-gather(bf16[24,512]{1,0:T(8,128)(2,1)} %param.15), channel_id=1, replica_groups=mesh['req'=32,'tp'=8] {'req'}, dimensions={0}, use_global_device_ids=true | all-gather | bytes 811008 | tf_op jit(solution)/shard_map/all_gather | solution.py:131
  36.8 50.0 %while.18 = (s32[]{:T(128)}, f32[64,1,4]{0,2,1:T(4,128)S(1)}, f32[64,1,4]{0,2,1:T(4,128)S(1)}, f32[64,1,4,128]{3,0,2,1:T(8,128)S(1)}, s32[2]{0:T(128)}, /*index=...) while((s32[]{:T(128)}, f32[64,1,4]{0,2,1:T(4,128)S(1)}, ...), condition=%wide.region_9.10_spmd.clone, body=%wide.region_6.9_spmd.clone.sunk | while | flops 136876160 | bytes 4351959 | solution.py:70
  37.8 1.4 fusion.83
  39.2 1.4 fusion.86
  43.4 1.4 fusion.86
  46.2 1.4 fusion.83
  47.6 1.4 fusion.86
  51.7 1.4 fusion.86
  55.9 1.4 fusion.86
  58.7 1.4 fusion.83
  60.1 1.4 fusion.86
  64.2 1.4 fusion.86
  68.4 1.4 fusion.86
  71.2 1.4 fusion.83
  72.6 1.4 fusion.86
  76.7 1.4 fusion.86
  80.9 1.4 fusion.86
  83.7 1.4 fusion.83
  85.0 1.4 fusion.86
  87.1 2.0 fusion.27
  90.8 109.1 %all-reduce = f32[768,4]{0,1:T(4,128)S(1)} all-reduce(f32[768,4]{0,1:T(4,128)S(1)} %fusion.26), channel_id=4, replica_groups=mesh['req'=32,'tp'=8] {'req'}, use_global_device_ids=true, to_apply=%region_11.12.clone | all-reduce | flops 3072 | bytes 24576
  203.2 3.6 %fusion.37 = f32[24,4096]{1,0:T(8,128)} fusion(bf16[512,4096]{1,0:T(8,128)(2,1)} %param.25, bf16[3,8,4,128]{3,2,1,0:T(4,128)(2,1)S(1)} %bitcast.95), kind=kOutput, calls=%fused_computation.57 | convolution fusion | flops 100663296 | bytes 4612096 | tf_op jit(solution)/shard_map/dot_general | solution.py:190
  206.9 60.7 %all-gather.3.cloned.1.call-done = f32[192,4096]{1,0:T(8,128)} async-done(((f32[24,4096]{1,0:T(8,128)}), f32[192,4096]{1,0:T(8,128)}) %all-gather.3.cloned.1.call-update) | async-done | bytes 3145744 | tf_op jit(solution)/shard_map/all_gather | solution.py:15
  267.5 2.1 reduce_sum.81
  (202 shorter events, 35.5 us)
Async XLA Ops:
  7.2 193.8 %copy-start = (bf16[24,128,128]{2,1,0:T(8,128)(2,1)S(1)}, bf16[24,128,128]{2,1,0:T(8,128)(2,1)}, u32[]{:S(2)}) copy-start(bf16[24,128,128]{2,1,0:T(8,128)(2,1)} %param.20) | copy-start | bytes 2359300
  7.2 194.7 %reduce-scatter.3.cloned.1.call-start = ((), (), s32[]{:S(2)}) async-start(), calls=%async_computation.1 | async-start | bytes 1622016 | tf_op jit(solution)/shard_map/reduce_scatter | solution.py:143
  86.8 2.4 copy-start.2
  86.9 2.4 copy-start.7
  86.9 113.9 %copy-start.4 = (bf16[24,128]{1,0:T(8,128)(2,1)S(1)}, bf16[24,128]{1,0:T(8,128)(2,1)}, u32[]{:S(2)}) copy-start(bf16[24,128]{1,0:T(8,128)(2,1)} %param.17) | copy-start | bytes 18436
  86.9 114.0 %copy-start.6 = (bf16[24,128]{1,0:T(8,128)(2,1)S(1)}, bf16[24,128]{1,0:T(8,128)(2,1)}, u32[]{:S(2)}) copy-start(bf16[24,128]{1,0:T(8,128)(2,1)} %param.16) | copy-start | bytes 18436
  86.9 115.9 %copy-start.5 = (bf16[24,128,128]{2,1,0:T(8,128)(2,1)S(1)}, bf16[24,128,128]{2,1,0:T(8,128)(2,1)}, u32[]{:S(2)}) copy-start(bf16[24,128,128]{2,1,0:T(8,128)(2,1)} %param.21) | copy-start | bytes 2359300
  89.2 178.3 %all-gather.3.cloned.1.call-start = ((), (), s32[]{:S(2)}) async-start(), calls=%async_computation.2 | async-start | bytes 3538944 | tf_op jit(solution)/shard_map/all_gather | solution.py:15
  202.8 4.1 %copy-start.3 = (bf16[4096]{0:T(1024)(128)(2,1)S(1)}, bf16[4096]{0:T(1024)(128)(2,1)}, u32[]{:S(2)}) copy-start(bf16[4096]{0:T(1024)(128)(2,1)} %param.27) | copy-start | bytes 24580
  203.2 66.5 %copy-start.1 = (bf16[24,4096]{1,0:T(8,128)(2,1)S(1)}, bf16[24,4096]{1,0:T(8,128)(2,1)}, u32[]{:S(2)}) copy-start(bf16[24,4096]{1,0:T(8,128)(2,1)} %param.26) | copy-start | bytes 589828
Sparse Core Ops, SparseCore 0:
  89.3 86.8 reduce-scatter.2
  207.0 60.5 all-gather.2
